TPU v7x, 32 devices: a whole 2x2x4 slice. The times are simulated.
32 devices in a mesh: expert: 4 (over z), shard: 8 (over y, x, core).
Axes of the slice: x: 2, y: 2, z: 4, core: 2. Of those that a mesh axis runs over, the one named last changes fastest.
Arguments:
- tokens: bfloat16 [18912, 768], P(('expert', 'shard')), may hold values from -6 to 6
- image_counts: int32 [4, 8], P('expert', 'shard'), may hold values from 1 to 3, as said below
- routes: int32 [18912, 2], P(('expert', 'shard')), may hold values from 0 to 3, all different within a row; in each aligned block of 591 rows (0 to 590, 591 to 1181, ...) at most 376 rows name the same one
- w_qkv: bfloat16 [768, 2304], P('shard'), may hold values from -0.21875 to 0.21875
- w_out: bfloat16 [768, 768], P('shard'), may hold values from -1.5 to 1.5
- w_router: bfloat16 [768, 4], P('shard'), may hold values from -0.15625 to 0.15625
- gain_attn: bfloat16 [768], P('shard'), may hold values from 0.25 to 1.75
- gain_moe: bfloat16 [768], P('shard'), may hold values from 0.25 to 1.75
- w_in: bfloat16 [4, 768, 3072], P('expert', 'shard'), may hold values from -0.21875 to 0.21875
- w_back: bfloat16 [4, 3072, 768], P('expert', 'shard'), may hold values from -0.625 to 0.625
- cotangent: bfloat16 [18912, 768], P(('expert', 'shard')), may hold values from -6 to 6
Outputs:
- output: bfloat16 [18912, 768], P(('expert', 'shard'))
- grad_tokens: bfloat16 [18912, 768], P(('expert', 'shard'))
- grad_w_qkv: float32 [768, 2304], P('shard')
- grad_w_out: float32 [768, 768], P('shard')
- grad_w_router: float32 [768, 4], P('shard')
- grad_gain_attn: float32 [768], P('shard')
- grad_gain_moe: float32 [768], P('shard')
- grad_w_in: float32 [4, 768, 3072], P('expert', 'shard')
- grad_w_back: float32 [4, 3072, 768], P('expert', 'shard')
Inputs may be any that keep to these rules, and one draw needn't show every extreme that they name: `image_counts`: each device holds between 1 and 3 live images; some device holds 3 and some holds 1. `routes`: the two experts of a token differ; among the rows of one device at most 376 name any one expert.
All inputs are finite; a program needn't handle non-finite values.
Results may differ from a plain program's by a relative error of at most 0.024.
Values may be sent and summed in bfloat16 or wider, within the bound.
No kernel may reach another device: no remote copies, remote signals or barrier semaphores. Data moves between devices by JAX's collectives and lax.ppermute only.
A program may use at most 256 MiB of HBM per device.

v0:
```python
import jax
import jax.numpy as jnp
from jax import lax
from jax.sharding import PartitionSpec as P

H = 12
HD = 64
SEQ = 197
EPSILON = 1e-06
ROW_CONTRACT = (((0,), (0,)), ((), ()))
COL_CONTRACT = (((1,), (1,)), ((), ()))


def layer_norm(values, norm_gain):
    row_mean = jnp.mean(values, axis=-1, keepdims=True)
    centered = values - row_mean
    variance = jnp.mean(centered * centered, axis=-1, keepdims=True)
    return centered * lax.rsqrt(variance + EPSILON) * norm_gain


def normalize_rows(scores):
    row_top = jnp.max(scores, axis=-1, keepdims=True)
    exp_scores = jnp.exp(scores - row_top)
    return exp_scores / jnp.sum(exp_scores, axis=-1, keepdims=True)


def gelu_exact(values):
    return jax.nn.gelu(values, approximate=False)


def shards(
    tokens,
    image_counts,
    routes,
    w_qkv,
    w_out,
    w_router,
    gain_attn,
    gain_moe,
    w_in,
    w_back,
    cotangent,
):
    rows, width = tokens.shape
    experts = lax.axis_size("expert")
    capacity = 8 * (5 * rows // (16 * experts)) + 8
    overflow = experts * capacity
    images = rows // SEQ
    score_scale = HD ** (-0.5)
    row_ids = jnp.arange(rows, dtype=jnp.int32)
    live_int = (row_ids // SEQ < image_counts[0, 0]).astype(jnp.int32)
    live_rows = live_int.astype(jnp.float32)
    full_qkv, full_out, full_router, full_gain_attn, full_gain_moe = (
        lax.all_gather(w_qkv, "shard", axis=0, tiled=True),
        lax.all_gather(w_out, "shard", axis=0, tiled=True),
        lax.all_gather(w_router, "shard", axis=0, tiled=True),
        lax.all_gather(gain_attn, "shard", axis=0, tiled=True),
        lax.all_gather(gain_moe, "shard", axis=0, tiled=True),
    )
    gain_one = full_gain_attn.astype(jnp.float32)
    gain_two = full_gain_moe.astype(jnp.float32)
    gathered = (
        lax.all_gather(w_in, "shard", axis=1, tiled=True),
        lax.all_gather(w_back, "shard", axis=1, tiled=True),
    )
    expert_first = gathered[0][0]
    expert_second = gathered[1][0]
    token_f = tokens.astype(jnp.float32)
    attn_in = layer_norm(token_f, gain_one).astype(jnp.bfloat16)
    projected = jnp.dot(attn_in, full_qkv, preferred_element_type=jnp.float32).astype(jnp.bfloat16)
    split_heads = projected.reshape(images, SEQ, 3, H, HD)
    queries = split_heads[:, :, 0]
    keys_part = split_heads[:, :, 1]
    values_part = split_heads[:, :, 2]
    scores = (
        jnp.einsum("ishd,ithd->ihst", queries, keys_part, preferred_element_type=jnp.float32)
        * score_scale
    )
    row_top = jnp.max(scores, axis=-1, keepdims=True)
    log_total = row_top + jnp.log(jnp.sum(jnp.exp(scores - row_top), axis=-1, keepdims=True))
    attn_probs = jnp.exp(scores - log_total)
    mixed_rows = (
        jnp.einsum(
            "ihst,ithd->ishd",
            attn_probs.astype(jnp.bfloat16),
            values_part,
            preferred_element_type=jnp.float32,
        )
        .reshape(rows, width)
        .astype(jnp.bfloat16)
    )
    hidden_state = token_f + jnp.dot(mixed_rows, full_out, preferred_element_type=jnp.float32)
    moe_in = layer_norm(hidden_state, gain_two).astype(jnp.bfloat16)
    logits = jnp.dot(moe_in, full_router, preferred_element_type=jnp.float32)
    router_probs = normalize_rows(logits)
    expert_ids = jnp.arange(experts, dtype=jnp.int32)
    choose = (routes[:, :, None] == expert_ids).astype(jnp.float32)
    chosen = jnp.sum(choose * router_probs[:, None, :], axis=2)
    pick_table = (routes[:, :, None] == expert_ids).astype(jnp.int32) * live_int[:, None, None]
    flat_picks = pick_table.reshape(rows * 2, experts)
    before = jnp.cumsum(flat_picks, axis=0) - flat_picks
    slot_index = jnp.sum(before * flat_picks, axis=1).reshape(rows, 2)
    position = jnp.where(live_int[:, None] > 0, routes * capacity + slot_index, overflow)
    safe_index = jnp.minimum(position, overflow - 1)
    outgoing = jnp.zeros((overflow, width), jnp.bfloat16)
    outgoing = (
        outgoing.at[position[:, 0]]
        .set(moe_in, mode="drop")
        .at[position[:, 1]]
        .set(moe_in, mode="drop")
    )
    outgoing = outgoing.reshape(experts, capacity, width)
    arrived = lax.all_to_all(outgoing, "expert", split_axis=0, concat_axis=0, tiled=True)
    sources = arrived.shape[0]
    slot_count = arrived.shape[1]
    flat_rows = arrived.reshape(sources * slot_count, width)
    pre_act = jnp.dot(flat_rows, expert_first, preferred_element_type=jnp.float32)
    activated = gelu_exact(pre_act).astype(jnp.bfloat16)
    produced = jnp.dot(activated, expert_second, preferred_element_type=jnp.float32).astype(
        jnp.bfloat16
    )
    produced, pre_act, activated, arrived = (
        produced.reshape(sources, slot_count, width),
        pre_act.reshape(sources, slot_count, -1),
        activated.reshape(sources, slot_count, -1),
        arrived,
    )
    returned = lax.all_to_all(produced, "expert", split_axis=0, concat_axis=0, tiled=True)
    picked = returned.reshape(overflow, width)[safe_index].astype(jnp.float32)
    weighted = chosen * live_rows[:, None]
    moe_out = jnp.sum(weighted[:, :, None] * picked, axis=1)
    output = (live_rows[:, None] * (hidden_state + moe_out)).astype(jnp.bfloat16)
    grad_out = cotangent.astype(jnp.float32) * live_rows[:, None]
    grad_chosen = jnp.sum(grad_out[:, None, :] * picked, axis=2) * live_rows[:, None]
    grad_picked = (weighted[:, :, None] * grad_out[:, None, :]).astype(jnp.bfloat16)
    back_out = jnp.zeros((overflow, width), jnp.bfloat16)
    back_out = (
        back_out.at[position[:, 0]]
        .set(grad_picked[:, 0], mode="drop")
        .at[position[:, 1]]
        .set(grad_picked[:, 1], mode="drop")
    )
    arriving_grad = lax.all_to_all(
        back_out.reshape(experts, capacity, width),
        "expert",
        split_axis=0,
        concat_axis=0,
        tiled=True,
    )
    regathered = (
        lax.all_gather(w_in, "shard", axis=1, tiled=True),
        lax.all_gather(w_back, "shard", axis=1, tiled=True),
    )
    back_first = regathered[0][0]
    back_second = regathered[1][0]
    flat_grad = arriving_grad.reshape(overflow, width)
    flat_pre = pre_act.reshape(overflow, -1)
    flat_act = activated.reshape(overflow, -1)
    flat_arrived = arrived.reshape(overflow, width)
    grad_second = lax.dot_general(
        flat_act, flat_grad, ROW_CONTRACT, preferred_element_type=jnp.float32
    )
    hidden_grad = lax.dot_general(
        flat_grad, back_second, COL_CONTRACT, preferred_element_type=jnp.float32
    )
    gelu_value, gelu_back = jax.vjp(gelu_exact, flat_pre)
    pre_grad = gelu_back(hidden_grad)[0].astype(jnp.bfloat16)
    grad_first = lax.dot_general(
        flat_arrived, pre_grad, ROW_CONTRACT, preferred_element_type=jnp.float32
    )
    row_grad = lax.dot_general(
        pre_grad, back_first, COL_CONTRACT, preferred_element_type=jnp.float32
    ).astype(jnp.bfloat16)
    back_rows = lax.all_to_all(
        row_grad.reshape(experts, capacity, width),
        "expert",
        split_axis=0,
        concat_axis=0,
        tiled=True,
    )
    incoming = back_rows.reshape(overflow, width)[safe_index].astype(jnp.float32)
    expert_part = jnp.sum(incoming, axis=1) * live_rows[:, None]
    prob_sum = jnp.sum(choose * grad_chosen[:, :, None], axis=1)
    logit_grad = (
        router_probs * (prob_sum - jnp.sum(router_probs * prob_sum, axis=-1, keepdims=True))
    ).astype(jnp.bfloat16)
    grad_router = lax.dot_general(
        moe_in, logit_grad, ROW_CONTRACT, preferred_element_type=jnp.float32
    )
    moe_in_grad = expert_part + lax.dot_general(
        logit_grad, full_router, COL_CONTRACT, preferred_element_type=jnp.float32
    )
    norm_value, norm_back = jax.vjp(layer_norm, hidden_state, gain_two)
    state_part, grad_gain_two = norm_back(moe_in_grad)
    state_grad = grad_out + state_part
    branch_grad = state_grad.astype(jnp.bfloat16)
    grad_wout = lax.dot_general(
        mixed_rows, branch_grad, ROW_CONTRACT, preferred_element_type=jnp.float32
    )
    mixed_grad = lax.dot_general(
        branch_grad, full_out, COL_CONTRACT, preferred_element_type=jnp.float32
    )
    mixed_grad = mixed_grad.astype(jnp.bfloat16).reshape(images, SEQ, H, HD)
    again_scores = (
        jnp.einsum("ishd,ithd->ihst", queries, keys_part, preferred_element_type=jnp.float32)
        * score_scale
    )
    again_probs = jnp.exp(again_scores - log_total)
    grad_values = jnp.einsum(
        "ihst,ishd->ithd",
        again_probs.astype(jnp.bfloat16),
        mixed_grad,
        preferred_element_type=jnp.float32,
    )
    prob_grad = jnp.einsum(
        "ishd,ithd->ihst", mixed_grad, values_part, preferred_element_type=jnp.float32
    )
    score_grad = (
        again_probs * (prob_grad - jnp.sum(again_probs * prob_grad, axis=-1, keepdims=True))
    ).astype(jnp.bfloat16)
    grad_queries = (
        jnp.einsum("ihst,ithd->ishd", score_grad, keys_part, preferred_element_type=jnp.float32)
        * score_scale
    )
    grad_keys = (
        jnp.einsum("ihst,ishd->ithd", score_grad, queries, preferred_element_type=jnp.float32)
        * score_scale
    )
    projected_grad = (
        jnp.stack([grad_queries, grad_keys, grad_values], axis=2)
        .reshape(rows, 3 * width)
        .astype(jnp.bfloat16)
    )
    grad_qkv = lax.dot_general(
        attn_in, projected_grad, ROW_CONTRACT, preferred_element_type=jnp.float32
    )
    attn_in_grad = lax.dot_general(
        projected_grad, full_qkv, COL_CONTRACT, preferred_element_type=jnp.float32
    )
    first_value, first_back = jax.vjp(layer_norm, token_f, gain_one)
    token_part, grad_gain_one = first_back(attn_in_grad)
    grad_tokens = (state_grad + token_part).astype(jnp.bfloat16)
    grad_in_share, grad_back_share = (
        lax.psum_scatter(
            grad_first[None].astype(jnp.bfloat16), "shard", scatter_dimension=1, tiled=True
        ).astype(jnp.float32),
        lax.psum_scatter(
            grad_second[None].astype(jnp.bfloat16), "shard", scatter_dimension=1, tiled=True
        ).astype(jnp.float32),
    )
    shares = (
        lax.psum_scatter(
            grad_qkv.astype(jnp.bfloat16), "shard", scatter_dimension=0, tiled=True
        ).astype(jnp.float32),
        lax.psum_scatter(
            grad_wout.astype(jnp.bfloat16), "shard", scatter_dimension=0, tiled=True
        ).astype(jnp.float32),
        lax.psum_scatter(
            grad_router.astype(jnp.bfloat16), "shard", scatter_dimension=0, tiled=True
        ).astype(jnp.float32),
        lax.psum_scatter(
            grad_gain_one.astype(jnp.bfloat16), "shard", scatter_dimension=0, tiled=True
        ).astype(jnp.float32),
        lax.psum_scatter(
            grad_gain_two.astype(jnp.bfloat16), "shard", scatter_dimension=0, tiled=True
        ).astype(jnp.float32),
    )
    totals = (
        lax.psum(shares[0].astype(jnp.bfloat16), "expert").astype(jnp.float32),
        lax.psum(shares[1].astype(jnp.bfloat16), "expert").astype(jnp.float32),
        lax.psum(shares[2].astype(jnp.bfloat16), "expert").astype(jnp.float32),
        lax.psum(shares[3].astype(jnp.bfloat16), "expert").astype(jnp.float32),
        lax.psum(shares[4].astype(jnp.bfloat16), "expert").astype(jnp.float32),
    )
    return (
        output,
        grad_tokens,
        totals[0],
        totals[1],
        totals[2],
        totals[3],
        totals[4],
        grad_in_share,
        grad_back_share,
    )


def solution(mesh):
    return jax.shard_map(
        shards,
        mesh=mesh,
        in_specs=(
            P(("expert", "shard"), None),
            P("expert", "shard"),
            P(("expert", "shard"), None),
            P("shard", None),
            P("shard", None),
            P("shard", None),
            P("shard"),
            P("shard"),
            P("expert", "shard", None),
            P("expert", "shard", None),
            P(("expert", "shard"), None),
        ),
        out_specs=(
            P(("expert", "shard"), None),
            P(("expert", "shard"), None),
            P("shard", None),
            P("shard", None),
            P("shard", None),
            P("shard"),
            P("shard"),
            P("expert", "shard", None),
            P("expert", "shard", None),
        ),
        check_vma=False,
    )
```

profile of v0, /device:TPU:0, one launch (start us, length us, event | category | flops | bytes accessed | tf_op | source)
XLA Modules:
  0.0 760.9 jit_solution(17173408247433804776)
XLA Ops:
  9.4 1.3 fusion.75
  13.1 15.5 %all-reduce.6 = (bf16[768]{0:T(1024)(128)(2,1)S(1)}, bf16[768]{0:T(1024)(128)(2,1)S(1)}) all-reduce(bf16[768]{0:T(1024)(128)(2,1)S(1)} %dynamic-update-slice, bf16[768]{0:T(1024)(128)(2,1)S(1)} %dynamic-update-slice.1), channel_id=1, replica_groups=mesh['expert'=4,'shard'=8] {'shard'}, use_global_device_ids=true, to_apply=%add.1 | all-reduce | flops 1536 | bytes 6144
  34.2 12.4 %all-gather.6.cloned.1.call-done = bf16[768,2304]{1,0:T(8,128)(2,1)} async-done(((bf16[96,2304]{1,0:T(8,128)(2,1)}), bf16[768,2304]{1,0:T(8,128)(2,1)}) %all-gather.6.cloned.1.call-update) | async-done | bytes 3538960 | tf_op jit(solution)/shard_map/all_gather | solution.py:54
  46.6 6.0 convolution_convert_fusion.3
  52.6 9.3 %reshape.295 = bf16[3,197,3,12,64]{4,3,2,1,0:T(8,128)(2,1)} reshape(bf16[591,2304]{1,0:T(8,128)(2,1)} %convolution_convert_fusion.3) | data formatting | bytes 5446656 | tf_op jit(solution)/shard_map/reshape | solution.py:71
  61.8 6.7 fusion.74
  68.5 4.2 copy.146
  72.7 4.2 copy.147
  76.9 3.5 copy.145
  80.4 3.4 multiply_reduce_fusion.1
  83.9 1.6 exponential_reduce_fusion
  87.4 1.6 fusion.34
  90.0 2.1 convert_element_type.167
  92.1 2.6 fusion.76
  95.0 8.0 %scatter_custom_fusion = bf16[1504,768]{1,0:T(8,128)(2,1)} fusion(s32[591]{0:T(1024)S(1)} %get-tuple-element.16, bf16[]{:T(256)} %constant.53.clone.1, f32[591,768]{1,0:T(8,128)S(1)} %get-tuple-element.42, f32[768]{0:T(1024)S(1)} %convert_element_type.168, f32[591]{0:T(1024)S(1)} %fusion.63, f32[591]{0:T(1024)S(1)} %broadcast_multiply_fusion.2), kind=kCustom, calls=%fused_computation.92 | custom fusion | flops 1815552 | bytes 4141058 | tf_op jit(solution)/shard_map/scatter | solution.py:108
  103.1 9.9 %scatter_custom_fusion.1 = bf16[1504,768]{1,0:T(8,128)(2,1)} fusion(bf16[1504,768]{1,0:T(8,128)(2,1)} %scatter_custom_fusion, s32[591]{0:T(1024)S(1)} %get-tuple-element.15, f32[591,768]{1,0:T(8,128)S(1)} %get-tuple-element.42, f32[768]{0:T(1024)S(1)} %convert_element_type.168, f32[591]{0:T(1024)S(1)} %fusion.63, f32[591]{0:T(1024)S(1)} %broadcast_multiply_fusion.2), kind=kCustom, calls=%fused_computation.155 | custom fusion | flops 1815552 | bytes 4141056 | tf_op jit(solution)/shard_map/scatter | solution.py:110
  113.0 4.6 all-to-all-start
  118.2 52.6 %all-to-all-done = bf16[4,376,768]{2,1,0:T(8,128)(2,1)S(1)} async-done(((bf16[4,376,768]{2,1,0:T(8,128)(2,1)}), bf16[4,376,768]{2,1,0:T(8,128)(2,1)S(1)}, u32[]{:S(2)}, u32[]{:S(2)}) %all-to-all-start) | async-done | bytes 2310176 | tf_op jit(solution)/shard_map/all_to_all | solution.py:113
  170.8 47.9 %multiply_convert_fusion = (bf16[1504,3072]{1,0:T(8,128)(2,1)}, f32[1504,3072]{1,0:T(8,128)}, f32[1504,3072]{1,0:T(8,128)}) fusion(bf16[1504,768]{1,0:T(8,128)(2,1)S(1)} %bitcast.123, bf16[1,768,3072]{2,1,0:T(8,128)(2,1)} %all-gather.10.cloned.1.call-done), kind=kOutput, calls=%fused_computation.9 | convolution fusion | flops 7397081088 | bytes 53231616 | tf_op jit(solution)/shard_map/dot_general | solution.py:117
  218.7 12.3 %fusion.19 = bf16[1504,768]{1,0:T(8,128)(2,1)} fusion(bf16[1504,3072]{1,0:T(8,128)(2,1)} %get-tuple-element.30, bf16[1,3072,768]{2,1,0:T(8,128)(2,1)} %all-gather.12.cloned.1.call-done), kind=kOutput, calls=%fused_computation.47 | convolution fusion | flops 7097917440 | bytes 16269312 | tf_op jit(solution)/shard_map/dot_general | solution.py:119
  231.0 3.8 all-to-all-start.1
  234.8 9.4 %all-gather = bf16[8,96,4]{1,2,0:T(4,128)(2,1)S(1)} all-gather(bf16[1,96,4]{1,2,0:T(4,128)(2,1)S(1)} %bitcast.131), channel_id=1, replica_groups=mesh['expert'=4,'shard'=8] {'shard'}, dimensions={0}, use_global_device_ids=true | all-gather | bytes 6912 | tf_op jit(solution)/shard_map/all_gather | solution.py:56
  246.8 1.5 convert_multiply_fusion
  249.1 38.0 %all-to-all-done.1 = bf16[4,376,768]{2,1,0:T(8,128)(2,1)S(1)} async-done(((bf16[4,376,768]{2,1,0:T(8,128)(2,1)}), bf16[4,376,768]{2,1,0:T(8,128)(2,1)S(1)}, u32[]{:S(2)}, u32[]{:S(2)}) %all-to-all-start.1) | async-done | bytes 2310176 | tf_op jit(solution)/shard_map/all_to_all | solution.py:128
  287.0 4.8 gather_fusion
  291.9 5.2 reshape.277
  297.0 5.6 multiply_reduce_fusion.2
  302.7 6.9 scatter_custom_fusion.2
  309.6 7.5 scatter_custom_fusion.3
  317.2 55.0 %all_to_all.20 = bf16[4,376,768]{2,1,0:T(8,128)(2,1)S(1)} all-to-all(bf16[4,376,768]{2,1,0:T(8,128)(2,1)S(1)} %bitcast.122), channel_id=1, replica_groups=mesh['expert'=4,'shard'=8] {'expert'}, dimensions={0} | all-to-all | bytes 4620288 | tf_op jit(solution)/shard_map/all_to_all | solution.py:143
  372.1 23.0 %add_convert_fusion = bf16[1504,3072]{1,0:T(8,128)(2,1)} fusion(f32[1504,3072]{1,0:T(8,128)} %get-tuple-element.31, f32[1504,3072]{1,0:T(8,128)} %get-tuple-element.43, bf16[1504,768]{1,0:T(8,128)(2,1)S(1)} %bitcast.125, bf16[1,3072,768]{2,1,0:T(8,128)(2,1)} %all-gather.12.cloned.1.call-done), kind=kOutput, calls=%fused_computation.8 | convolution fusion | flops 7161446400 | bytes 53231616 | tf_op jit(solution)/shard_map/dot_general | solution.py:163
  395.1 12.4 %fusion.16 = bf16[1504,768]{1,0:T(8,128)(2,1)} fusion(bf16[1504,3072]{1,0:T(8,128)(2,1)} %add_convert_fusion, bf16[1,768,3072]{2,1,0:T(8,128)(2,1)} %all-gather.10.cloned.1.call-done), kind=kOutput, calls=%fused_computation.46 | convolution fusion | flops 7097917440 | bytes 16269312 | tf_op jit(solution)/shard_map/dot_general | solution.py:171
  407.5 3.6 all-to-all-start.3
  412.4 50.7 %all-to-all-done.3 = bf16[4,376,768]{2,1,0:T(8,128)(2,1)S(1)} async-done(((bf16[4,376,768]{2,1,0:T(8,128)(2,1)}), bf16[4,376,768]{2,1,0:T(8,128)(2,1)S(1)}, u32[]{:S(2)}, u32[]{:S(2)}) %all-to-all-start.3) | async-done | bytes 2310176 | tf_op jit(solution)/shard_map/all_to_all | solution.py:174
  463.2 4.8 gather_fusion.1
  468.0 5.0 reshape.278
  473.1 7.7 %reduce_sum.190 = f32[591,768]{1,0:T(8,128)} reduce(f32[591,2,768]{2,1,0:T(2,128)} %reshape.278, f32[]{:T(128)} %constant.48.clone.1), dimensions={1}, to_apply=%region_17.18 | reduce | flops 453888 | bytes 5446660 | tf_op jit(solution)/shard_map/reduce_sum | solution.py:182
  480.8 2.6 multiply_reduce_fusion.4
  483.4 1.8 fusion.72
  487.4 2.9 reshape.296
  490.3 4.7 copy.129
  495.1 6.1 multiply_reduce_fusion
  501.2 3.6 multiply_convert_fusion.1
  504.8 2.3 convolution_convert_fusion.6
  507.3 3.0 fusion.32
  512.0 4.8 fusion.35
  517.8 5.6 copy.134
  523.4 10.1 %convert_element_type.183 = bf16[591,2304]{0,1:T(8,128)(2,1)} reshape(bf16[3,197,3,12,64]{1,0,4,3,2:T(4,128)(2,1)} %copy.134) | data formatting | bytes 5446656 | tf_op jit(solution)/shard_map/convert_element_type | solution.py:232
  533.5 6.8 convolution_convert_fusion.1
  540.4 1.6 copy-done.21
  542.0 13.3 %fusion.15 = bf16[1,3072,768]{2,1,0:T(8,128)(2,1)} fusion(bf16[1504,3072]{1,0:T(8,128)(2,1)} %get-tuple-element.30, bf16[1504,768]{1,0:T(8,128)(2,1)S(1)} %bitcast.126), kind=kOutput, calls=%fused_computation.41 | convolution fusion | flops 7099121664 | bytes 16269312 | tf_op jit(solution)/shard_map/dot_general | solution.py:160
  555.4 1.8 copy-done.19
  557.2 13.2 %fusion.14 = bf16[1,768,3072]{2,1,0:T(8,128)(2,1)} fusion(bf16[1504,768]{1,0:T(8,128)(2,1)S(1)} %bitcast.124, bf16[1504,3072]{1,0:T(8,128)(2,1)} %add_convert_fusion), kind=kOutput, calls=%fused_computation.40 | convolution fusion | flops 7099121664 | bytes 16269312 | tf_op jit(solution)/shard_map/dot_general | solution.py:168
  572.1 5.7 fusion.31
  578.8 12.6 %all-reduce.5 = (bf16[768]{0:T(1024)(128)(2,1)S(1)}, bf16[768]{0:T(1024)(128)(2,1)S(1)}) all-reduce(bf16[768]{0:T(1024)(128)(2,1)S(1)} %get-tuple-element.13, bf16[768]{0:T(1024)(128)(2,1)S(1)} %get-tuple-element.9), channel_id=5, replica_groups=mesh['expert'=4,'shard'=8] {'shard'}, use_global_device_ids=true, to_apply=%region_33.34.clone | all-reduce | flops 1536 | bytes 6144
  591.5 9.4 %all-reduce.7 = (bf16[96,4]{0,1:T(4,128)(2,1)S(1)}, bf16[96]{0:T(256)(128)(2,1)S(1)}, bf16[96]{0:T(256)(128)(2,1)S(1)}) all-reduce(bf16[96,4]{0,1:T(4,128)(2,1)S(1)} %copy.140, bf16[96]{0:T(256)(128)(2,1)S(1)} %dynamic-slice.3, bf16[96]{0:T(256)(128)(2,1)S(1)} %dynamic-slice.5), channel_id=1, replica_groups=mesh['expert'=4,'shard'=8] {'expert'}, use_global_device_ids=true, to_apply=%region_31.32 | all-reduce | flops 576 | bytes 2304 | tf_op jit(solution)/shard_map/psum | solution.py:271
  602.5 3.1 add_convert_fusion.1
  605.6 45.3 %reduce-scatter.14.cloned.1.call-done = bf16[1,384,768]{2,1,0:T(8,128)(2,1)} async-done(((bf16[1,3072,768]{2,1,0:T(8,128)(2,1)}), bf16[1,384,768]{2,1,0:T(8,128)(2,1)}) %reduce-scatter.14.cloned.1.call-update) | async-done | bytes 589840 | tf_op jit(solution)/shard_map/reduce_scatter | solution.py:247
  650.9 2.2 convert_element_type.200
  653.1 55.1 %reduce-scatter.12.cloned.1.call-done = bf16[1,96,3072]{2,1,0:T(8,128)(2,1)} async-done(((bf16[1,768,3072]{2,1,0:T(8,128)(2,1)}), bf16[1,96,3072]{2,1,0:T(8,128)(2,1)}) %reduce-scatter.12.cloned.1.call-update) | async-done | bytes 589840 | tf_op jit(solution)/shard_map/reduce_scatter | solution.py:244
  708.2 2.2 convert_element_type.197
  710.4 39.9 %all-reduce.11.cloned.1.call-done = (bf16[96,2304]{1,0:T(8,128)(2,1)}, bf16[96,768]{1,0:T(8,128)(2,1)}) async-done(((bf16[96,2304]{1,0:T(8,128)(2,1)}, bf16[96,768]{1,0:T(8,128)(2,1)}), (bf16[96,2304]{1,0:T(8,128)(2,1)}, bf16[96,768]{1,0:T(8,128)(2,1)})) %all-reduce.11.cloned.1.call-update) | async-done | bytes 589840 | tf_op jit(solution)/shard_map/psum | solution.py:269
  750.2 2.0 convert_element_type.186
  752.2 1.6 convert_element_type.188
  (188 shorter events, 26.2 us)
Async XLA Ops:
  7.2 25.7 %copy-start.31 = (s32[591,2]{0,1:T(2,128)S(1)}, s32[591,2]{0,1:T(2,128)}, u32[]{:S(2)}) copy-start(s32[591,2]{0,1:T(2,128)} %param.13) | copy-start | bytes 14188
  7.2 26.3 %copy-start.5 = (bf16[591,768]{1,0:T(8,128)(2,1)S(1)}, bf16[591,768]{1,0:T(8,128)(2,1)}, u32[]{:S(2)}) copy-start(bf16[591,768]{1,0:T(8,128)(2,1)} %param.11) | copy-start | bytes 2723332
  7.2 39.4 %all-gather.6.cloned.1.call-start = ((), (), s32[]{:S(2)}) async-start(), calls=%async_computation.9 | async-start | bytes 3981312 | tf_op jit(solution)/shard_map/all_gather | solution.py:54
  7.9 84.1 %all-gather.8.cloned.1.call-start = ((), (), s32[]{:S(2)}) async-start(), calls=%async_computation.10 | async-start | bytes 1327104 | tf_op jit(solution)/shard_map/all_gather | solution.py:55
  8.7 109.5 %all-gather.10.cloned.1.call-start = ((), (), s32[]{:S(2)}) async-start(), calls=%async_computation.11 | async-start | bytes 5308416 | tf_op jit(solution)/shard_map/all_gather | solution.py:63
  28.6 23.9 %copy-start.39 = (f32[768]{0:T(1024)}, f32[768]{0:T(1024)S(1)}, u32[]{:S(2)}) copy-start(f32[768]{0:T(1024)S(1)} %convert_element_type.161) | copy-start | bytes 9220
  28.6 74.4 %copy-start.27 = (f32[768]{0:T(1024)}, f32[768]{0:T(1024)S(1)}, u32[]{:S(2)}) copy-start(f32[768]{0:T(1024)S(1)} %convert_element_type.168) | copy-start | bytes 9220
  33.5 61.5 %copy-start.44 = (s32[591]{0:T(1024)}, s32[591]{0:T(1024)S(1)}, u32[]{:S(2)}) copy-start(s32[591]{0:T(1024)S(1)} %get-tuple-element.16) | copy-start | bytes 7096
  33.5 69.5 %copy-start.43 = (s32[591]{0:T(1024)}, s32[591]{0:T(1024)S(1)}, u32[]{:S(2)}) copy-start(s32[591]{0:T(1024)S(1)} %get-tuple-element.15) | copy-start | bytes 7096
  33.8 18.8 %copy-start.33 = (f32[591]{0:T(1024)}, f32[591]{0:T(1024)S(1)}, u32[]{:S(2)}) copy-start(f32[591]{0:T(1024)S(1)} %broadcast_multiply_fusion.3) | copy-start | bytes 7096
  34.2 18.4 %copy-start.35 = (f32[591]{0:T(1024)}, f32[591]{0:T(1024)S(1)}, u32[]{:S(2)}) copy-start(f32[591]{0:T(1024)S(1)} %fusion.30) | copy-start | bytes 7096
  34.2 18.4 %copy-start.41 = (f32[591]{0:T(1024)}, f32[591]{0:T(1024)S(1)}, u32[]{:S(2)}) copy-start(f32[591]{0:T(1024)S(1)} %fusion.62) | copy-start | bytes 7096
  80.4 5.1 copy-start.7
  83.9 2.9 copy-start
  86.8 0.6 copy-start.22
  94.6 8.4 %copy-start.1 = (f32[591,768]{1,0:T(8,128)}, f32[591,768]{1,0:T(8,128)S(1)}, u32[]{:S(2)}) copy-start(f32[591,768]{1,0:T(8,128)S(1)} %get-tuple-element.42) | copy-start | bytes 5446660
  94.7 8.4 %copy-start.25 = (f32[591]{0:T(1024)}, f32[591]{0:T(1024)S(1)}, u32[]{:S(2)}) copy-start(f32[591]{0:T(1024)S(1)} %broadcast_multiply_fusion.2) | copy-start | bytes 7096
  95.0 18.0 %copy-start.37 = (f32[591]{0:T(1024)}, f32[591]{0:T(1024)S(1)}, u32[]{:S(2)}) copy-start(f32[591]{0:T(1024)S(1)} %multiply_reduce_fusion.6) | copy-start | bytes 7096
  95.0 18.0 %copy-start.29 = (f32[591]{0:T(1024)}, f32[591]{0:T(1024)S(1)}, u32[]{:S(2)}) copy-start(f32[591]{0:T(1024)S(1)} %fusion.63) | copy-start | bytes 7096
  113.0 57.8 %all-to-all-start = ((bf16[4,376,768]{2,1,0:T(8,128)(2,1)}), bf16[4,376,768]{2,1,0:T(8,128)(2,1)S(1)}, u32[]{:S(2)}, u32[]{:S(2)}) async-start(bf16[4,376,768]{2,1,0:T(8,128)(2,1)} %bitcast.121), calls=%async_computation | async-start | bytes 4620288 | tf_op jit(solution)/shard_map/all_to_all | solution.py:113
  117.6 101.1 %all-gather.12.cloned.1.call-start = ((), (), s32[]{:S(2)}) async-start(), calls=%async_computation.12 | async-start | bytes 5308416 | tf_op jit(solution)/shard_map/all_gather | solution.py:64
  170.8 47.9 %copy-start.18 = (bf16[4,376,768]{2,1,0:T(8,128)(2,1)}, bf16[4,376,768]{2,1,0:T(8,128)(2,1)S(1)}, u32[]{:S(2)}) copy-start(bf16[4,376,768]{2,1,0:T(8,128)(2,1)S(1)} %all-to-all-done) | copy-start | bytes 6930436
  231.0 3.8 copy-start.45
  231.0 15.8 %copy-start.15 = (bf16[591,768]{1,0:T(8,128)(2,1)S(1)}, bf16[591,768]{1,0:T(8,128)(2,1)}, u32[]{:S(2)}) copy-start(bf16[591,768]{1,0:T(8,128)(2,1)} %param.21) | copy-start | bytes 2723332
  231.0 56.1 %all-to-all-start.1 = ((bf16[4,376,768]{2,1,0:T(8,128)(2,1)}), bf16[4,376,768]{2,1,0:T(8,128)(2,1)S(1)}, u32[]{:S(2)}, u32[]{:S(2)}) async-start(bf16[4,376,768]{2,1,0:T(8,128)(2,1)} %bitcast.128), calls=%async_computation.1 | async-start | bytes 4620288 | tf_op jit(solution)/shard_map/all_to_all | solution.py:128
  234.7 13.6 %copy-start.26 = (f32[591]{0:T(1024)S(1)}, f32[591]{0:T(1024)}, u32[]{:S(2)}) copy-start(f32[591]{0:T(1024)} %copy-done.25) | copy-start | bytes 7096
  234.8 13.6 %copy-start.28 = (f32[768]{0:T(1024)S(1)}, f32[768]{0:T(1024)}, u32[]{:S(2)}) copy-start(f32[768]{0:T(1024)} %copy-done.27) | copy-start | bytes 9220
  234.8 13.5 %copy-start.30 = (f32[591]{0:T(1024)S(1)}, f32[591]{0:T(1024)}, u32[]{:S(2)}) copy-start(f32[591]{0:T(1024)} %copy-done.29) | copy-start | bytes 7096
  245.9 2.4 copy-start.2
  248.3 0.7 copy-start.32
  291.9 5.2 copy-start.13
  372.1 23.0 %copy-start.20 = (bf16[4,376,768]{2,1,0:T(8,128)(2,1)}, bf16[4,376,768]{2,1,0:T(8,128)(2,1)S(1)}, u32[]{:S(2)}) copy-start(bf16[4,376,768]{2,1,0:T(8,128)(2,1)S(1)} %all_to_all.20) | copy-start | bytes 6930436
  407.5 55.7 %all-to-all-start.3 = ((bf16[4,376,768]{2,1,0:T(8,128)(2,1)}), bf16[4,376,768]{2,1,0:T(8,128)(2,1)S(1)}, u32[]{:S(2)}, u32[]{:S(2)}) async-start(bf16[4,376,768]{2,1,0:T(8,128)(2,1)} %bitcast.127), calls=%async_computation.3 | async-start | bytes 4620288 | tf_op jit(solution)/shard_map/all_to_all | solution.py:174
  411.1 160.2 %reduce-scatter.16.cloned.1.call-start = ((), (), s32[]{:S(2)}) async-start(), calls=%async_computation.17 | async-start | bytes 221184
  412.4 190.1 %reduce-scatter.10.cloned.1.call-start = ((), (), s32[]{:S(2)}) async-start(), calls=%async_computation.14 | async-start | bytes 1327104 | tf_op jit(solution)/shard_map/reduce_scatter | solution.py:255
  473.1 7.7 %copy-start.3 = (f32[591,768]{1,0:T(8,128)S(1)}, f32[591,768]{1,0:T(8,128)}, u32[]{:S(2)}) copy-start(f32[591,768]{1,0:T(8,128)} %copy-done.1) | copy-start | bytes 5446660
  480.8 2.6 copy-start.38
  480.8 2.6 copy-start.14
  483.4 3.0 copy-start.16
  483.4 3.0 copy-start.46
  485.2 1.2 copy-start.11
  490.3 4.7 copy-start.23
  490.3 10.9 %slice-start = ((s8[7372800]{0:T(1024)(128)(4,1)}), s8[3178496]{0:T(1024)(128)(4,1)S(1)}, s32[]{:S(2)}) async-start(s8[7372800]{0:T(1024)(128)(4,1)} %bitcast.117), calls=%async_computation.19 | async-start | bytes 6356992
  495.1 6.1 slice-start.1
  501.2 3.6 copy-start.12
  501.2 3.6 copy-start.17
  501.2 3.6 copy-start.24
  504.8 2.4 copy-start.10
  507.2 3.1 copy-start.9
  507.2 95.3 %reduce-scatter.8.cloned.1.call-start = ((), (), s32[]{:S(2)}) async-start(), calls=%async_computation.13 | async-start | bytes 3981312 | tf_op jit(solution)/shard_map/reduce_scatter | solution.py:252
  507.2 3.5 copy-start.4
  510.7 1.3 copy-start.8
  523.4 10.1 %copy-start.6 = (bf16[591,768]{1,0:T(8,128)(2,1)S(1)}, bf16[591,768]{1,0:T(8,128)(2,1)}, u32[]{:S(2)}) copy-start(bf16[591,768]{1,0:T(8,128)(2,1)} %param.11) | copy-start | bytes 2723332
  523.4 10.1 %copy-start.34 = (f32[591]{0:T(1024)S(1)}, f32[591]{0:T(1024)}, u32[]{:S(2)}) copy-start(f32[591]{0:T(1024)} %copy-done.33) | copy-start | bytes 7096
  523.4 10.1 %copy-start.40 = (f32[768]{0:T(1024)S(1)}, f32[768]{0:T(1024)}, u32[]{:S(2)}) copy-start(f32[768]{0:T(1024)} %copy-done.39) | copy-start | bytes 9220
  523.4 10.1 %copy-start.42 = (f32[591]{0:T(1024)S(1)}, f32[591]{0:T(1024)}, u32[]{:S(2)}) copy-start(f32[591]{0:T(1024)} %copy-done.41) | copy-start | bytes 7096
  540.3 1.7 copy-start.21
  540.3 110.6 %reduce-scatter.14.cloned.1.call-start = ((), (), s32[]{:S(2)}) async-start(), calls=%async_computation.16 | async-start | bytes 5308416 | tf_op jit(solution)/shard_map/reduce_scatter | solution.py:247
  555.3 1.8 copy-start.19
  555.4 152.8 %reduce-scatter.12.cloned.1.call-start = ((), (), s32[]{:S(2)}) async-start(), calls=%async_computation.15 | async-start | bytes 5308416 | tf_op jit(solution)/shard_map/reduce_scatter | solution.py:244
  570.4 179.9 %all-reduce.11.cloned.1.call-start = ((), (), s32[]{:S(2)}) async-start(), calls=%async_computation.18 | async-start | bytes 1179648 | tf_op jit(solution)/shard_map/psum | solution.py:269
  572.1 5.7 copy-start.36
Sparse Core Ops, SparseCore 0:
  9.9 36.6 all-gather.5
  48.5 23.9 all-gather.7
  74.3 38.7 all-gather.9
  119.9 39.2 all-gather.11
  415.2 34.1 reduce-scatter.15
  507.3 34.8 reduce-scatter.9
  545.6 48.0 reduce-scatter.7
  597.2 53.7 reduce-scatter.13
  654.4 53.7 reduce-scatter.11
  710.5 39.7 all-reduce.10
where the time goes:
time: 769 us; the launch traced here: 761 us
  waiting for transfers between devices  297 us (39%)
  matrix products  170 us (22%)
  local copies, waits for them, and re-layouts  104 us (14%)
  blocking collectives  102 us (13%)
  other arithmetic  58.9 us (8%)
  between operations  17.1 us (2%)
  starting transfers between devices  12.6 us (2%)
    reduce_scatter x1, waiting for transfers between devices, shards(): lax.psum_scatter(grad_first[None].astype(jnp.bfloat16), 'shard', scatter_...  55.1 us
    all_to_all x1, blocking collectives, shards(): lax.all_to_all(back_out.reshape(experts, capacity, width), 'expert', spli...  55 us
    all_to_all x1, waiting for transfers between devices, shards(): lax.all_to_all(outgoing, 'expert', split_axis=0, concat_axis=0, tiled=True)  52.6 us
    all_to_all x1, waiting for transfers between devices, shards(): lax.all_to_all(row_grad.reshape(experts, capacity, width), 'expert', spli...  50.7 us
    dot_general x1, matrix products, shards(): jnp.dot(flat_rows, expert_first, preferred_element_type=jnp.float32)  47.9 us
    reduce_scatter x1, waiting for transfers between devices, shards(): lax.psum_scatter(grad_second[None].astype(jnp.bfloat16), 'shard', scatter...  45.3 us
    psum x1, waiting for transfers between devices, shards(): lax.psum(shares[0].astype(jnp.bfloat16), 'expert').astype(jnp.float32)  39.9 us
    all_to_all x1, waiting for transfers between devices, shards(): lax.all_to_all(produced, 'expert', split_axis=0, concat_axis=0, tiled=True)  38 us
  transfers between devices with their start and end apart: 13, of which 7 were waited for; matrix products, arithmetic and copies ran while one was open for 32% of the time, Pallas kernels for 0%

commit v1 on v0

--- a/solution.py
+++ b/solution.py
@@ -1,3 +1,4 @@
+import functools
 import jax
 import jax.numpy as jnp
 from jax import lax
@@ -9,6 +10,15 @@
 EPSILON = 1e-06
 ROW_CONTRACT = (((0,), (0,)), ((), ()))
 COL_CONTRACT = (((1,), (1,)), ((), ()))
+
+
+def review_the_digits(array_here, chip_axis):
+    earlier = jax.lax.all_gather(array_here, chip_axis)
+    all_values = jnp.sum(earlier, axis=0)
+    return all_values
+
+
+apply_pieces_all_on_mesh = functools.partial(review_the_digits, chip_axis="expert")
 
 
 def layer_norm(values, norm_gain):
@@ -266,7 +276,7 @@
         ).astype(jnp.float32),
     )
     totals = (
-        lax.psum(shares[0].astype(jnp.bfloat16), "expert").astype(jnp.float32),
+        apply_pieces_all_on_mesh(shares[0].astype(jnp.bfloat16)).astype(jnp.float32),
         lax.psum(shares[1].astype(jnp.bfloat16), "expert").astype(jnp.float32),
         lax.psum(shares[2].astype(jnp.bfloat16), "expert").astype(jnp.float32),
         lax.psum(shares[3].astype(jnp.bfloat16), "expert").astype(jnp.float32),

time: 769 us -> 841 us (1.094)
  waiting for transfers between devices: 297 us -> 367 us
    all_gather x0 -> x1, waiting for transfers between devices: none -> 39.7 us  [review_the_digits(): earlier = jax.lax.all_gather(array_here, chip_axis)]
    psum x1, waiting for transfers between devices: 39.9 us -> 0.42 us  [shards(): lax.psum(shares[1].astype(jnp.bfloat16), 'expert').astype(jnp.float32)]
    unnamed x11 -> x12, waiting for transfers between devices: 2.73 us -> 40 us
    reduce_scatter x1, waiting for transfers between devices: 0.01 us -> 21.9 us  [shards(): lax.psum_scatter(grad_qkv.astype(jnp.bfloat16), 'shard', scatter_dimensio...]
    reduce_scatter x1, waiting for transfers between devices: 45.3 us -> 55.6 us  [shards(): lax.psum_scatter(grad_second[None].astype(jnp.bfloat16), 'shard', scatter...]
    unnamed x113 -> x107, local copies, waits for them, and re-layouts: 24.7 us -> 24.8 us
  transfers between devices with their start and end apart: 13 -> 14, of which waited for: 7 -> 10; matrix products, arithmetic and copies ran while one was open for 32% -> 24% of each run, Pallas kernels for 0% -> 0%
where the time goes in v1:
time: 841 us; the launch traced here: 833 us
  waiting for transfers between devices  367 us (44%)
  matrix products  168 us (20%)
  blocking collectives  104 us (12%)
  local copies, waits for them, and re-layouts  103 us (12%)
  other arithmetic  62.4 us (7%)
  between operations  16.7 us (2%)
  starting transfers between devices  12.4 us (1%)
    reduce_scatter x1, waiting for transfers between devices, shards(): lax.psum_scatter(grad_second[None].astype(jnp.bfloat16), 'shard', scatter...  55.6 us
    all_to_all x1, blocking collectives, shards(): lax.all_to_all(back_out.reshape(experts, capacity, width), 'expert', spli...  55 us
    reduce_scatter x1, waiting for transfers between devices, shards(): lax.psum_scatter(grad_first[None].astype(jnp.bfloat16), 'shard', scatter_...  54.9 us
    all_to_all x1, waiting for transfers between devices, shards(): lax.all_to_all(outgoing, 'expert', split_axis=0, concat_axis=0, tiled=True)  52.6 us
    all_to_all x1, waiting for transfers between devices, shards(): lax.all_to_all(row_grad.reshape(experts, capacity, width), 'expert', spli...  51.9 us
    dot_general x1, matrix products, shards(): jnp.dot(flat_rows, expert_first, preferred_element_type=jnp.float32)  47.9 us
    unnamed x12, waiting for transfers between devices  40 us
    all_gather x1, waiting for transfers between devices, review_the_digits(): earlier = jax.lax.all_gather(array_here, chip_axis)  39.7 us
  transfers between devices with their start and end apart: 14, of which 10 were waited for; matrix products, arithmetic and copies ran while one was open for 24% of the time, Pallas kernels for 0%

profile of v1, /device:TPU:0, one launch (start us, length us, event | category | flops | bytes accessed | tf_op | source)
XLA Modules:
  0.0 833.3 jit_solution(9011812009175649418)
XLA Ops:
  13.1 15.5 %all-reduce.6 = (bf16[768]{0:T(1024)(128)(2,1)S(1)}, bf16[768]{0:T(1024)(128)(2,1)S(1)}) all-reduce(bf16[768]{0:T(1024)(128)(2,1)S(1)} %dynamic-update-slice, bf16[768]{0:T(1024)(128)(2,1)S(1)} %dynamic-update-slice.1), channel_id=1, replica_groups=mesh['expert'=4,'shard'=8] {'shard'}, use_global_device_ids=true, to_apply=%add.1 | all-reduce | flops 1536 | bytes 6144
  34.2 12.4 %all-gather.8.cloned.1.call-done = bf16[768,2304]{1,0:T(8,128)(2,1)} async-done(((bf16[96,2304]{1,0:T(8,128)(2,1)}), bf16[768,2304]{1,0:T(8,128)(2,1)}) %all-gather.8.cloned.1.call-update) | async-done | bytes 3538960 | tf_op jit(solution)/shard_map/all_gather | solution.py:64
  46.6 6.0 convolution_convert_fusion.3
  52.6 9.3 %reshape.296 = bf16[3,197,3,12,64]{4,3,2,1,0:T(8,128)(2,1)} reshape(bf16[591,2304]{1,0:T(8,128)(2,1)} %convolution_convert_fusion.3) | data formatting | bytes 5446656 | tf_op jit(solution)/shard_map/reshape | solution.py:81
  61.8 6.7 fusion.74
  68.5 4.2 copy.146
  72.7 4.2 copy.147
  76.9 3.5 copy.145
  80.4 3.4 multiply_reduce_fusion.1
  83.9 1.6 exponential_reduce_fusion
  87.4 1.6 fusion.34
  90.0 2.1 convert_element_type.169
  92.1 2.6 fusion.76
  95.0 8.0 scatter_custom_fusion
  103.1 9.9 %scatter_custom_fusion.1 = bf16[1504,768]{1,0:T(8,128)(2,1)} fusion(bf16[1504,768]{1,0:T(8,128)(2,1)} %scatter_custom_fusion, s32[591]{0:T(1024)S(1)} %get-tuple-element.15, f32[591,768]{1,0:T(8,128)S(1)} %get-tuple-element.40, f32[768]{0:T(1024)S(1)} %convert_element_type.170, f32[591]{0:T(1024)S(1)} %fusion.63, f32[591]{0:T(1024)S(1)} %broadcast_multiply_fusion.2), kind=kCustom, calls=%fused_computation.155 | custom fusion | flops 1815552 | bytes 4141056 | tf_op jit(solution)/shard_map/scatter | solution.py:120
  113.0 4.6 all-to-all-start
  118.2 52.6 %all-to-all-done = bf16[4,376,768]{2,1,0:T(8,128)(2,1)S(1)} async-done(((bf16[4,376,768]{2,1,0:T(8,128)(2,1)}), bf16[4,376,768]{2,1,0:T(8,128)(2,1)S(1)}, u32[]{:S(2)}, u32[]{:S(2)}) %all-to-all-start) | async-done | bytes 2310176 | tf_op jit(solution)/shard_map/all_to_all | solution.py:123
  170.8 47.9 %multiply_convert_fusion = (bf16[1504,3072]{1,0:T(8,128)(2,1)}, f32[1504,3072]{1,0:T(8,128)}, f32[1504,3072]{1,0:T(8,128)}) fusion(bf16[1504,768]{1,0:T(8,128)(2,1)S(1)} %bitcast.124, bf16[1,768,3072]{2,1,0:T(8,128)(2,1)} %all-gather.12.cloned.1.call-done), kind=kOutput, calls=%fused_computation.9 | convolution fusion | flops 7397081088 | bytes 53231616 | tf_op jit(solution)/shard_map/dot_general | solution.py:127
  218.7 12.3 %fusion.19 = bf16[1504,768]{1,0:T(8,128)(2,1)} fusion(bf16[1504,3072]{1,0:T(8,128)(2,1)} %get-tuple-element.28, bf16[1,3072,768]{2,1,0:T(8,128)(2,1)} %all-gather.14.cloned.1.call-done), kind=kOutput, calls=%fused_computation.47 | convolution fusion | flops 7097917440 | bytes 16269312 | tf_op jit(solution)/shard_map/dot_general | solution.py:129
  231.0 3.8 all-to-all-start.1
  234.8 9.4 %all-gather.1 = bf16[8,96,4]{1,2,0:T(4,128)(2,1)S(1)} all-gather(bf16[1,96,4]{1,2,0:T(4,128)(2,1)S(1)} %bitcast.133), channel_id=1, replica_groups=mesh['expert'=4,'shard'=8] {'shard'}, dimensions={0}, use_global_device_ids=true | all-gather | bytes 6912 | tf_op jit(solution)/shard_map/all_gather | solution.py:66
  246.8 1.5 convert_multiply_fusion
  249.6 37.5 %all-to-all-done.1 = bf16[4,376,768]{2,1,0:T(8,128)(2,1)S(1)} async-done(((bf16[4,376,768]{2,1,0:T(8,128)(2,1)}), bf16[4,376,768]{2,1,0:T(8,128)(2,1)S(1)}, u32[]{:S(2)}, u32[]{:S(2)}) %all-to-all-start.1) | async-done | bytes 2310176 | tf_op jit(solution)/shard_map/all_to_all | solution.py:138
  287.0 4.8 gather_fusion
  291.9 5.2 reshape.278
  297.0 5.6 multiply_reduce_fusion.2
  302.7 6.9 scatter_custom_fusion.2
  309.6 7.5 scatter_custom_fusion.3
  317.2 55.0 %all_to_all.20 = bf16[4,376,768]{2,1,0:T(8,128)(2,1)S(1)} all-to-all(bf16[4,376,768]{2,1,0:T(8,128)(2,1)S(1)} %bitcast.123), channel_id=1, replica_groups=mesh['expert'=4,'shard'=8] {'expert'}, dimensions={0} | all-to-all | bytes 4620288 | tf_op jit(solution)/shard_map/all_to_all | solution.py:153
  372.1 23.0 %add_convert_fusion = bf16[1504,3072]{1,0:T(8,128)(2,1)} fusion(f32[1504,3072]{1,0:T(8,128)} %get-tuple-element.29, f32[1504,3072]{1,0:T(8,128)} %get-tuple-element.41, bf16[1504,768]{1,0:T(8,128)(2,1)S(1)} %bitcast.126, bf16[1,3072,768]{2,1,0:T(8,128)(2,1)} %all-gather.14.cloned.1.call-done), kind=kOutput, calls=%fused_computation.8 | convolution fusion | flops 7161446400 | bytes 53231616 | tf_op jit(solution)/shard_map/dot_general | solution.py:173
  395.2 12.4 %fusion.16 = bf16[1504,768]{1,0:T(8,128)(2,1)} fusion(bf16[1504,3072]{1,0:T(8,128)(2,1)} %add_convert_fusion, bf16[1,768,3072]{2,1,0:T(8,128)(2,1)} %all-gather.12.cloned.1.call-done), kind=kOutput, calls=%fused_computation.46 | convolution fusion | flops 7097917440 | bytes 16269312 | tf_op jit(solution)/shard_map/dot_general | solution.py:181
  407.5 3.6 all-to-all-start.3
  411.3 51.9 %all-to-all-done.3 = bf16[4,376,768]{2,1,0:T(8,128)(2,1)S(1)} async-done(((bf16[4,376,768]{2,1,0:T(8,128)(2,1)}), bf16[4,376,768]{2,1,0:T(8,128)(2,1)S(1)}, u32[]{:S(2)}, u32[]{:S(2)}) %all-to-all-start.3) | async-done | bytes 2310176 | tf_op jit(solution)/shard_map/all_to_all | solution.py:184
  463.2 4.8 gather_fusion.1
  468.0 5.0 reshape.279
  473.1 7.7 reduce_sum.204
  480.8 2.6 multiply_reduce_fusion.4
  483.4 1.8 fusion.72
  486.4 2.3 convolution_convert_fusion.6
  488.7 3.4 convolution_convert_fusion.7
  492.2 3.0 reshape.297
  495.2 3.1 copy.129
  498.3 8.8 %multiply_reduce_fusion = (f32[3,12,197]{2,1,0:T(8,128)S(1)}, f32[3,12,197,197]{2,3,1,0:T(8,128)}) fusion(f32[3,12,197,197]{2,3,1,0:T(8,128)} %copy-done, f32[3,12,197]{2,1,0:T(8,128)S(1)} %copy-done.20, bf16[3,197,12,64]{1,3,2,0:T(8,128)(2,1)} %copy.129, bf16[3,197,1,12,64]{1,4,3,0,2:T(8,128)(2,1)} %copy-done.6), kind=kOutput, calls=%fused_computation.24 | convolution fusion | flops 184413264 | bytes 13049280 | tf_op jit(solution)/shard_map/ishd,ithd->ihst/dot_general | solution.py:225
  507.3 6.5 multiply_convert_fusion.1
  516.5 1.4 fusion.35
  518.7 5.6 copy.134
  524.3 9.9 %convert_element_type.185 = bf16[591,2304]{0,1:T(8,128)(2,1)} reshape(bf16[3,197,3,12,64]{1,0,4,3,2:T(4,128)(2,1)} %copy.134) | data formatting | bytes 5446656 | tf_op jit(solution)/shard_map/convert_element_type | solution.py:242
  534.3 6.8 convolution_convert_fusion.1
  544.2 12.5 %fusion.15 = bf16[1,3072,768]{2,1,0:T(8,128)(2,1)} fusion(bf16[1504,3072]{1,0:T(8,128)(2,1)} %get-tuple-element.28, bf16[1504,768]{1,0:T(8,128)(2,1)} %bitcast.127), kind=kOutput, calls=%fused_computation.41 | convolution fusion | flops 7099121664 | bytes 16269312 | tf_op jit(solution)/shard_map/dot_general | solution.py:170
  556.7 1.8 copy-done.17
  558.5 12.9 %fusion.14 = bf16[1,768,3072]{2,1,0:T(8,128)(2,1)} fusion(bf16[1504,768]{1,0:T(8,128)(2,1)S(1)} %bitcast.125, bf16[1504,3072]{1,0:T(8,128)(2,1)} %add_convert_fusion), kind=kOutput, calls=%fused_computation.40 | convolution fusion | flops 7099121664 | bytes 16269312 | tf_op jit(solution)/shard_map/dot_general | solution.py:178
  571.5 21.9 %reduce-scatter.8.cloned.1.call-done = bf16[96,2304]{1,0:T(8,128)(2,1)} async-done(((bf16[768,2304]{1,0:T(8,128)(2,1)}), bf16[96,2304]{1,0:T(8,128)(2,1)}) %reduce-scatter.8.cloned.1.call-update) | async-done | bytes 442384 | tf_op jit(solution)/shard_map/reduce_scatter | solution.py:262
  594.1 36.6 %reduce-scatter.16.cloned.1.call-done = bf16[96,4]{1,0:T(8,128)(2,1)} async-done(((bf16[768,4]{1,0:T(8,128)(2,1)}), bf16[96,4]{1,0:T(8,128)(2,1)}) %reduce-scatter.16.cloned.1.call-update) | async-done | bytes 784
  631.5 5.6 fusion.31
  638.1 12.5 %all-reduce.5 = (bf16[768]{0:T(1024)(128)(2,1)S(1)}, bf16[768]{0:T(1024)(128)(2,1)S(1)}) all-reduce(bf16[768]{0:T(1024)(128)(2,1)S(1)} %get-tuple-element.13, bf16[768]{0:T(1024)(128)(2,1)S(1)} %get-tuple-element.9), channel_id=6, replica_groups=mesh['expert'=4,'shard'=8] {'shard'}, use_global_device_ids=true, to_apply=%region_33.34.clone | all-reduce | flops 1536 | bytes 6144
  650.8 11.7 %all-reduce.7 = (bf16[96,4]{0,1:T(4,128)(2,1)S(1)}, bf16[96]{0:T(256)(128)(2,1)S(1)}, bf16[96]{0:T(256)(128)(2,1)S(1)}) all-reduce(bf16[96,4]{0,1:T(4,128)(2,1)S(1)} %copy.140, bf16[96]{0:T(256)(128)(2,1)S(1)} %dynamic-slice.3, bf16[96]{0:T(256)(128)(2,1)S(1)} %dynamic-slice.5), channel_id=1, replica_groups=mesh['expert'=4,'shard'=8] {'expert'}, use_global_device_ids=true, to_apply=%region_31.32 | all-reduce | flops 576 | bytes 2304 | tf_op jit(solution)/shard_map/psum | solution.py:281
  664.1 3.1 add_convert_fusion.1
  667.6 1.6 convert_element_type.190
  669.2 55.6 %reduce-scatter.14.cloned.1.call-done = bf16[1,384,768]{2,1,0:T(8,128)(2,1)} async-done(((bf16[1,3072,768]{2,1,0:T(8,128)(2,1)}), bf16[1,384,768]{2,1,0:T(8,128)(2,1)}) %reduce-scatter.14.cloned.1.call-update) | async-done | bytes 589840 | tf_op jit(solution)/shard_map/reduce_scatter | solution.py:257
  724.8 2.2 convert_element_type.202
  727.0 54.9 %reduce-scatter.12.cloned.1.call-done = bf16[1,96,3072]{2,1,0:T(8,128)(2,1)} async-done(((bf16[1,768,3072]{2,1,0:T(8,128)(2,1)}), bf16[1,96,3072]{2,1,0:T(8,128)(2,1)}) %reduce-scatter.12.cloned.1.call-update) | async-done | bytes 589840 | tf_op jit(solution)/shard_map/reduce_scatter | solution.py:254
  781.9 2.2 convert_element_type.199
  784.1 39.7 %all-gather.16.cloned.1.call-done = bf16[384,2304]{1,0:T(8,128)(2,1)} async-done(((bf16[96,2304]{1,0:T(8,128)(2,1)}), bf16[384,2304]{1,0:T(8,128)(2,1)}) %all-gather.16.cloned.1.call-update) | async-done | bytes 1769488 | tf_op jit(solution)/shard_map/all_gather | solution.py:16
  823.8 1.8 reduce_sum.250
  (186 shorter events, 30.7 us)
Async XLA Ops:
  7.2 25.7 %copy-start.28 = (s32[591,2]{0,1:T(2,128)S(1)}, s32[591,2]{0,1:T(2,128)}, u32[]{:S(2)}) copy-start(s32[591,2]{0,1:T(2,128)} %param.13) | copy-start | bytes 14188
  7.2 26.3 %copy-start.4 = (bf16[591,768]{1,0:T(8,128)(2,1)S(1)}, bf16[591,768]{1,0:T(8,128)(2,1)}, u32[]{:S(2)}) copy-start(bf16[591,768]{1,0:T(8,128)(2,1)} %param.11) | copy-start | bytes 2723332
  7.2 39.4 %all-gather.8.cloned.1.call-start = ((), (), s32[]{:S(2)}) async-start(), calls=%async_computation.9 | async-start | bytes 3981312 | tf_op jit(solution)/shard_map/all_gather | solution.py:64
  7.9 84.1 %all-gather.10.cloned.1.call-start = ((), (), s32[]{:S(2)}) async-start(), calls=%async_computation.10 | async-start | bytes 1327104 | tf_op jit(solution)/shard_map/all_gather | solution.py:65
  8.7 109.5 %all-gather.12.cloned.1.call-start = ((), (), s32[]{:S(2)}) async-start(), calls=%async_computation.11 | async-start | bytes 5308416 | tf_op jit(solution)/shard_map/all_gather | solution.py:73
  28.6 23.9 %copy-start.36 = (f32[768]{0:T(1024)}, f32[768]{0:T(1024)S(1)}, u32[]{:S(2)}) copy-start(f32[768]{0:T(1024)S(1)} %convert_element_type.163) | copy-start | bytes 9220
  28.6 74.4 %copy-start.24 = (f32[768]{0:T(1024)}, f32[768]{0:T(1024)S(1)}, u32[]{:S(2)}) copy-start(f32[768]{0:T(1024)S(1)} %convert_element_type.170) | copy-start | bytes 9220
  33.5 61.5 %copy-start.41 = (s32[591]{0:T(1024)}, s32[591]{0:T(1024)S(1)}, u32[]{:S(2)}) copy-start(s32[591]{0:T(1024)S(1)} %get-tuple-element.16) | copy-start | bytes 7096
  33.5 69.5 %copy-start.40 = (s32[591]{0:T(1024)}, s32[591]{0:T(1024)S(1)}, u32[]{:S(2)}) copy-start(s32[591]{0:T(1024)S(1)} %get-tuple-element.15) | copy-start | bytes 7096
  33.8 18.8 %copy-start.30 = (f32[591]{0:T(1024)}, f32[591]{0:T(1024)S(1)}, u32[]{:S(2)}) copy-start(f32[591]{0:T(1024)S(1)} %broadcast_multiply_fusion.3) | copy-start | bytes 7096
  34.2 18.4 %copy-start.32 = (f32[591]{0:T(1024)}, f32[591]{0:T(1024)S(1)}, u32[]{:S(2)}) copy-start(f32[591]{0:T(1024)S(1)} %fusion.30) | copy-start | bytes 7096
  34.2 18.4 %copy-start.38 = (f32[591]{0:T(1024)}, f32[591]{0:T(1024)S(1)}, u32[]{:S(2)}) copy-start(f32[591]{0:T(1024)S(1)} %fusion.62) | copy-start | bytes 7096
  80.4 5.1 copy-start.6
  83.9 2.9 copy-start
  86.8 0.6 copy-start.19
  94.6 8.4 %copy-start.1 = (f32[591,768]{1,0:T(8,128)}, f32[591,768]{1,0:T(8,128)S(1)}, u32[]{:S(2)}) copy-start(f32[591,768]{1,0:T(8,128)S(1)} %get-tuple-element.40) | copy-start | bytes 5446660
  94.7 8.4 %copy-start.22 = (f32[591]{0:T(1024)}, f32[591]{0:T(1024)S(1)}, u32[]{:S(2)}) copy-start(f32[591]{0:T(1024)S(1)} %broadcast_multiply_fusion.2) | copy-start | bytes 7096
  95.0 18.0 %copy-start.34 = (f32[591]{0:T(1024)}, f32[591]{0:T(1024)S(1)}, u32[]{:S(2)}) copy-start(f32[591]{0:T(1024)S(1)} %multiply_reduce_fusion.6) | copy-start | bytes 7096
  95.0 18.0 %copy-start.26 = (f32[591]{0:T(1024)}, f32[591]{0:T(1024)S(1)}, u32[]{:S(2)}) copy-start(f32[591]{0:T(1024)S(1)} %fusion.63) | copy-start | bytes 7096
  113.0 57.8 %all-to-all-start = ((bf16[4,376,768]{2,1,0:T(8,128)(2,1)}), bf16[4,376,768]{2,1,0:T(8,128)(2,1)S(1)}, u32[]{:S(2)}, u32[]{:S(2)}) async-start(bf16[4,376,768]{2,1,0:T(8,128)(2,1)} %bitcast.122), calls=%async_computation | async-start | bytes 4620288 | tf_op jit(solution)/shard_map/all_to_all | solution.py:123
  117.6 101.1 %all-gather.14.cloned.1.call-start = ((), (), s32[]{:S(2)}) async-start(), calls=%async_computation.12 | async-start | bytes 5308416 | tf_op jit(solution)/shard_map/all_gather | solution.py:74
  170.8 47.9 %copy-start.16 = (bf16[4,376,768]{2,1,0:T(8,128)(2,1)}, bf16[4,376,768]{2,1,0:T(8,128)(2,1)S(1)}, u32[]{:S(2)}) copy-start(bf16[4,376,768]{2,1,0:T(8,128)(2,1)S(1)} %all-to-all-done) | copy-start | bytes 6930436
  231.0 3.8 copy-start.42
  231.0 15.8 %copy-start.15 = (bf16[591,768]{1,0:T(8,128)(2,1)S(1)}, bf16[591,768]{1,0:T(8,128)(2,1)}, u32[]{:S(2)}) copy-start(bf16[591,768]{1,0:T(8,128)(2,1)} %param.21) | copy-start | bytes 2723332
  231.0 56.1 %all-to-all-start.1 = ((bf16[4,376,768]{2,1,0:T(8,128)(2,1)}), bf16[4,376,768]{2,1,0:T(8,128)(2,1)S(1)}, u32[]{:S(2)}, u32[]{:S(2)}) async-start(bf16[4,376,768]{2,1,0:T(8,128)(2,1)} %bitcast.128), calls=%async_computation.1 | async-start | bytes 4620288 | tf_op jit(solution)/shard_map/all_to_all | solution.py:138
  234.7 13.6 %copy-start.23 = (f32[591]{0:T(1024)S(1)}, f32[591]{0:T(1024)}, u32[]{:S(2)}) copy-start(f32[591]{0:T(1024)} %copy-done.22) | copy-start | bytes 7096
  234.7 13.6 %copy-start.25 = (f32[768]{0:T(1024)S(1)}, f32[768]{0:T(1024)}, u32[]{:S(2)}) copy-start(f32[768]{0:T(1024)} %copy-done.24) | copy-start | bytes 9220
  234.8 13.6 %copy-start.27 = (f32[591]{0:T(1024)S(1)}, f32[591]{0:T(1024)}, u32[]{:S(2)}) copy-start(f32[591]{0:T(1024)} %copy-done.26) | copy-start | bytes 7096
  245.9 2.4 copy-start.2
  248.3 0.7 copy-start.29
  248.6 0.9 copy-start.10
  291.9 5.2 copy-start.13
  372.1 23.0 %copy-start.18 = (bf16[4,376,768]{2,1,0:T(8,128)(2,1)}, bf16[4,376,768]{2,1,0:T(8,128)(2,1)S(1)}, u32[]{:S(2)}) copy-start(bf16[4,376,768]{2,1,0:T(8,128)(2,1)S(1)} %all_to_all.20) | copy-start | bytes 6930436
  407.5 55.7 %all-to-all-start.3 = ((bf16[4,376,768]{2,1,0:T(8,128)(2,1)}), bf16[4,376,768]{2,1,0:T(8,128)(2,1)S(1)}, u32[]{:S(2)}, u32[]{:S(2)}) async-start(bf16[4,376,768]{2,1,0:T(8,128)(2,1)} %bitcast.129), calls=%async_computation.3 | async-start | bytes 4620288 | tf_op jit(solution)/shard_map/all_to_all | solution.py:184
  411.2 132.3 %reduce-scatter.10.cloned.1.call-start = ((), (), s32[]{:S(2)}) async-start(), calls=%async_computation.14 | async-start | bytes 1327104 | tf_op jit(solution)/shard_map/reduce_scatter | solution.py:265
  473.1 7.7 copy-start.3
  480.8 2.6 copy-start.35
  480.8 2.6 copy-start.14
  483.4 3.0 copy-start.21
  485.2 1.2 copy-start.12
  486.4 2.3 copy-start.43
  495.2 3.1 copy-start.20
  498.3 18.1 %slice-start = ((s8[7372800]{0:T(1024)(128)(4,1)}), s8[3178496]{0:T(1024)(128)(4,1)S(1)}, s32[]{:S(2)}) async-start(s8[7372800]{0:T(1024)(128)(4,1)} %bitcast.118), calls=%async_computation.20 | async-start | bytes 6356992
  507.2 86.3 %reduce-scatter.8.cloned.1.call-start = ((), (), s32[]{:S(2)}) async-start(), calls=%async_computation.13 | async-start | bytes 3981312 | tf_op jit(solution)/shard_map/reduce_scatter | solution.py:262
  507.2 6.6 copy-start.9
  507.2 9.2 %slice-start.1 = ((s8[7372800]{0:T(1024)(128)(4,1)}), s8[4194304]{0:T(1024)(128)(4,1)S(1)}, s32[]{:S(2)}) async-start(s8[7372800]{0:T(1024)(128)(4,1)} %bitcast.118), calls=%async_computation.21 | async-start | bytes 8388608
  513.8 1.3 copy-start.8
  515.1 1.3 copy-start.7
  524.3 9.9 %copy-start.5 = (bf16[591,768]{1,0:T(8,128)(2,1)S(1)}, bf16[591,768]{1,0:T(8,128)(2,1)}, u32[]{:S(2)}) copy-start(bf16[591,768]{1,0:T(8,128)(2,1)} %param.11) | copy-start | bytes 2723332
  524.3 9.9 %copy-start.31 = (f32[591]{0:T(1024)S(1)}, f32[591]{0:T(1024)}, u32[]{:S(2)}) copy-start(f32[591]{0:T(1024)} %copy-done.30) | copy-start | bytes 7096
  524.3 9.9 %copy-start.37 = (f32[768]{0:T(1024)S(1)}, f32[768]{0:T(1024)}, u32[]{:S(2)}) copy-start(f32[768]{0:T(1024)} %copy-done.36) | copy-start | bytes 9220
  524.3 9.9 %copy-start.39 = (f32[591]{0:T(1024)S(1)}, f32[591]{0:T(1024)}, u32[]{:S(2)}) copy-start(f32[591]{0:T(1024)} %copy-done.38) | copy-start | bytes 7096
  541.1 1.2 copy-start.11
  541.1 89.6 %reduce-scatter.16.cloned.1.call-start = ((), (), s32[]{:S(2)}) async-start(), calls=%async_computation.19 | async-start | bytes 221184
  543.4 124.2 %all-reduce.10.cloned.1.call-start = ((), (), s32[]{:S(2)}) async-start(), calls=%async_computation.15 | async-start | bytes 294912 | tf_op jit(solution)/shard_map/psum | solution.py:280
  544.1 180.7 %reduce-scatter.14.cloned.1.call-start = ((), (), s32[]{:S(2)}) async-start(), calls=%async_computation.17 | async-start | bytes 5308416 | tf_op jit(solution)/shard_map/reduce_scatter | solution.py:257
  556.6 1.9 copy-start.17
  556.7 225.3 %reduce-scatter.12.cloned.1.call-start = ((), (), s32[]{:S(2)}) async-start(), calls=%async_computation.16 | async-start | bytes 5308416 | tf_op jit(solution)/shard_map/reduce_scatter | solution.py:254
  571.5 252.3 %all-gather.16.cloned.1.call-start = ((), (), s32[]{:S(2)}) async-start(), calls=%async_computation.18 | async-start | bytes 2211840 | tf_op jit(solution)/shard_map/all_gather | solution.py:16
  631.5 5.6 copy-start.33
Sparse Core Ops, SparseCore 0:
  9.9 36.6 all-gather.7
  48.5 23.9 all-gather.9
  74.3 38.7 all-gather.11
  119.9 39.2 all-gather.13
  507.3 34.8 reduce-scatter.9
  545.5 47.9 reduce-scatter.7
  597.1 33.6 reduce-scatter.15
  633.0 34.4 all-reduce.9
  671.0 53.7 reduce-scatter.13
  728.1 53.7 reduce-scatter.11
  783.5 40.2 all-gather.15
